TPU v7x, 512 devices: a whole 4x8x8 slice. The times are simulated.
512 devices in a mesh: req: 64 (over z, x, core), voc: 8 (over y).
Axes of the slice: x: 4, y: 8, z: 8, core: 2. Of those that a mesh axis runs over, the one named last changes fastest.
Arguments:
- hidden: bfloat16 [65536, 1600], P(('req', 'voc')), may hold values from -60 to 60
- norm_gain: float32 [1600], replicated, may hold values from 0.25 to 1.75
- unembed: bfloat16 [16384, 1600], P(('req', 'voc')), may hold values from -2 to 2
- targets: int32 [65536], P(('req', 'voc')), may hold values from 0 to 16383
- live: int32 [65536], P(('req', 'voc')), may hold values from 0 to 1, as said below
Outputs:
- logprob: float32 [65536], P(('req', 'voc'))
- entropy: float32 [65536], P(('req', 'voc'))
Inputs may be any that keep to these rules, and one draw needn't show every extreme that they name: Within each aligned block of 1024 slots (one owner's) the live slots form a prefix of 128 to 1024 slots, and in every draw at least one block is wholly live.
All inputs are finite; a program needn't handle non-finite values.
Results may differ from a plain program's by a relative error of at most 0.0067.
Values may be sent and summed in bfloat16 or wider, within the bound.
No kernel may reach another device: no remote copies, remote signals or barrier semaphores. Data moves between devices by JAX's collectives and lax.ppermute only.
A program may use at most 64 MiB of HBM per device.

v0:
```python
import jax
import jax.numpy as jnp
from jax import lax
from jax.sharding import Mesh, PartitionSpec as P

FLAT = ("z", "x", "c", "y")


def combine_stats(first, second):
    top = jnp.maximum(first[0], second[0])
    scale_one = jnp.exp(first[0] - top)
    scale_two = jnp.exp(second[0] - top)
    total = first[1] * scale_one + second[1] * scale_two
    spread = scale_one * (first[2] + (first[0] - top) * first[1]) + scale_two * (
        second[2] + (second[0] - top) * second[1]
    )
    return (top, total, spread, first[3] + second[3])


def shift(value, axis, size, step):
    return lax.ppermute(value, axis, [(i, (i + step) % size) for i in range(size)])


def chunk_stats(normed, piece, ids, wanted):
    logits = lax.dot_general(
        normed, piece, (((1,), (1,)), ((), ())), preferred_element_type=jnp.float32
    )
    chosen = jnp.sum(jnp.where(ids[None, :] == wanted[:, None], logits, 0.0), axis=1)
    fold_top = jnp.max(logits, axis=1)
    shifted = logits - fold_top[:, None]
    weights = jnp.exp(shifted)
    return (fold_top, jnp.sum(weights, axis=1), jnp.sum(weights * shifted, axis=1), chosen)


def on_device(hidden, norm_gain, unembed, targets, live):
    ny = lax.axis_size("y")
    nc = lax.axis_size("c")
    y = lax.axis_index("y")
    c = lax.axis_index("c")
    mine = hidden.shape[0]
    dim = hidden.shape[1]
    width = unembed.shape[0]
    wide = hidden.astype(jnp.float32)
    normed = (
        wide * lax.rsqrt(jnp.mean(wide * wide, axis=1, keepdims=True) + 1e-06) * norm_gain
    ).astype(jnp.bfloat16)
    code = jnp.zeros((mine, 16), jnp.bfloat16)
    code = code.at[:, 0].set((targets // 128).astype(jnp.bfloat16))
    code = code.at[:, 1].set((targets % 128).astype(jnp.bfloat16))
    block = jnp.concatenate([normed, code], axis=1)
    blocks = [None] * ny
    blocks[0] = block
    fwd = ny // 2
    cur = block
    for d in range(1, fwd + 1):
        cur = shift(cur, "y", ny, 1)
        blocks[ny - d] = cur
    cur = block
    for d in range(1, ny - fwd):
        cur = shift(cur, "y", ny, -1)
        blocks[d] = cur
    rows = jnp.concatenate([b[:, :dim] for b in blocks], axis=0)
    wanted = jnp.concatenate(
        [b[:, dim].astype(jnp.int32) * 128 + b[:, dim + 1].astype(jnp.int32) for b in blocks],
        axis=0,
    )
    whole = lax.all_gather(unembed, ("z", "x", "c"), axis=0, tiled=True)
    local = jnp.arange(whole.shape[0], dtype=jnp.int32)
    ids = (local // width * ny + y) * width + local % width
    count = rows.shape[0]
    zeros = jnp.zeros((count,), jnp.float32)
    stats = (jnp.full((count,), -1e30, jnp.float32), zeros, zeros, zeros)
    step = min(512, whole.shape[0])
    for first in range(0, whole.shape[0], step):
        stats = combine_stats(
            stats, chunk_stats(rows, whole[first : first + step], ids[first : first + step], wanted)
        )
    packed = jnp.roll(jnp.stack(stats).reshape(4, ny, mine), y, axis=1).reshape(4, ny * mine)
    got = lax.all_to_all(packed, "y", 1, 1, tiled=True).reshape(4, ny, mine)
    tops, totals, spreads, chosen = (got[0], got[1], got[2], got[3])
    top = jnp.max(tops, axis=0)
    scale = jnp.exp(tops - top[None])
    total = jnp.sum(totals * scale, axis=0)
    spread = jnp.sum(scale * (spreads + (tops - top[None]) * totals), axis=0)
    picked = jnp.sum(chosen, axis=0)
    mask = live.astype(jnp.float32)
    logprob = (picked - top - jnp.log(total)) * mask
    entropy = (jnp.log(total) - spread / total) * mask
    return (logprob, entropy)


def solution(mesh):
    nz, nx, nc = (8, 4, 2)
    ny = mesh.devices.shape[1]
    req = mesh.devices.shape[0]
    nz = req // (nx * nc)
    flat = Mesh(mesh.devices.reshape(nz, nx, nc, ny), FLAT)
    return jax.shard_map(
        on_device,
        mesh=flat,
        in_specs=(P(FLAT, None), P(), P(FLAT, None), P(FLAT), P(FLAT)),
        out_specs=(P(FLAT), P(FLAT)),
        check_vma=False,
    )
```

profile of v0, /device:TPU:1, one launch (start us, length us, event | category | flops | bytes accessed | tf_op | source)
XLA Modules:
  0.0 140.3 jit_solution(5805174977988451406)
XLA Ops:
  7.2 0.7 all-gather.2.cloned.1.call-update
  7.9 0.6 compare_reduce_fusion.1
  8.5 0.6 compare_reduce_fusion
  9.2 2.0 %broadcast_select_fusion = (bf16[128]{0:T(256)(128)(2,1)S(1)}, bf16[128,1]{0,1:T(2,128)(2,1)S(1)}) fusion(pred[]{:T(512)} %compare_reduce_fusion, s32[128]{0:T(128)} %param.12, pred[]{:T(512)} %compare_reduce_fusion.1), kind=kLoop, calls=%fused_computation.128 | loop fusion | flops 2944 | bytes 1026 | tf_op jit(solution)/shard_map/slice | solution.py:64
  11.2 1.2 fusion.12
  12.4 2.1 %constant_dynamic-update-slice_fusion = (bf16[1024,1600]{0,1:T(8,128)(2,1)}, bf16[128,1600]{0,1:T(8,128)(2,1)S(1)}) fusion(f32[1600]{0:T(1024)} %param.10, f32[128]{0:T(128)S(1)} %add_rsqrt_fusion, bf16[128,1600]{0,1:T(8,128)(2,1)} %param.9), kind=kLoop, calls=%fused_computation.45 | loop fusion | flops 819199 | bytes 1235712
  14.6 4.0 %collective-permute-start.3 = (bf16[128,1616]{0,1:T(8,128)(2,1)S(1)}, bf16[128,1616]{0,1:T(8,128)(2,1)S(1)}, u32[]{:S(2)}, u32[]{:S(2)}) collective-permute-start(bf16[128,1616]{0,1:T(8,128)(2,1)S(1)} %pad_maximum_fusion), channel_id=1, source_target_pairs={{0,1},{1,2},{2,3},{3,4},{4,5},{5,6},{6,7},{7,0},{8,9},{9,10},{10,1... | collective-permute-start | bytes 1241096 | tf_op jit(solution)/shard_map/ppermute | solution.py:21
  18.6 3.8 %collective-permute-start = (bf16[128,1616]{0,1:T(8,128)(2,1)S(1)}, bf16[128,1616]{0,1:T(8,128)(2,1)S(1)}, u32[]{:S(2)}, u32[]{:S(2)}) collective-permute-start(bf16[128,1616]{0,1:T(8,128)(2,1)S(1)} %pad_maximum_fusion), channel_id=1, source_target_pairs={{0,7},{1,0},{2,1},{3,2},{4,3},{5,4},{6,5},{7,6},{8,15},{9,8},{10,9... | collective-permute-start | bytes 1241096 | tf_op jit(solution)/shard_map/ppermute | solution.py:21
  22.5 3.4 %collective-permute-done.3 = bf16[128,1616]{0,1:T(8,128)(2,1)S(1)} collective-permute-done((bf16[128,1616]{0,1:T(8,128)(2,1)S(1)}, bf16[128,1616]{0,1:T(8,128)(2,1)S(1)}, u32[]{:S(2)}, u32[]{:S(2)}) %collective-permute-start.3) | collective-permute-done | bytes 413728 | tf_op jit(solution)/shard_map/ppermute | solution.py:21
  25.9 4.1 %collective-permute-start.4 = (bf16[128,1616]{0,1:T(8,128)(2,1)S(1)}, bf16[128,1616]{0,1:T(8,128)(2,1)S(1)}, u32[]{:S(2)}, u32[]{:S(2)}) collective-permute-start(bf16[128,1616]{0,1:T(8,128)(2,1)S(1)} %collective-permute-done.3), channel_id=1, source_target_pairs={{0,1},{1,2},{2,3},{3,4},{4,5},{5,6},{6,7},{7,0},{8,9},{9,10},{10,1... | collective-permute-start | bytes 1241096 | tf_op jit(solution)/shard_map/ppermute | solution.py:21
  30.0 4.7 %collective-permute-start.1 = (bf16[128,1616]{0,1:T(8,128)(2,1)S(1)}, bf16[128,1616]{0,1:T(8,128)(2,1)S(1)}, u32[]{:S(2)}, u32[]{:S(2)}) collective-permute-start(bf16[128,1616]{0,1:T(8,128)(2,1)S(1)} %collective-permute-done), channel_id=1, source_target_pairs={{0,7},{1,0},{2,1},{3,2},{4,3},{5,4},{6,5},{7,6},{8,15},{9,8},{10,9... | collective-permute-start | bytes 1241096 | tf_op jit(solution)/shard_map/ppermute | solution.py:21
  34.8 0.8 slice_dynamic-update-slice_fusion.6
  35.6 2.9 %collective-permute-done.4 = bf16[128,1616]{0,1:T(8,128)(2,1)S(1)} collective-permute-done((bf16[128,1616]{0,1:T(8,128)(2,1)S(1)}, bf16[128,1616]{0,1:T(8,128)(2,1)S(1)}, u32[]{:S(2)}, u32[]{:S(2)}) %collective-permute-start.4) | collective-permute-done | bytes 413728 | tf_op jit(solution)/shard_map/ppermute | solution.py:21
  38.5 2.9 %collective-permute-start.5 = (bf16[128,1616]{0,1:T(8,128)(2,1)S(1)}, bf16[128,1616]{0,1:T(8,128)(2,1)S(1)}, u32[]{:S(2)}, u32[]{:S(2)}) collective-permute-start(bf16[128,1616]{0,1:T(8,128)(2,1)S(1)} %collective-permute-done.4), channel_id=1, source_target_pairs={{0,1},{1,2},{2,3},{3,4},{4,5},{5,6},{6,7},{7,0},{8,9},{9,10},{10,1... | collective-permute-start | bytes 1241096 | tf_op jit(solution)/shard_map/ppermute | solution.py:21
  41.4 4.7 %collective-permute-start.2 = (bf16[128,1616]{0,1:T(8,128)(2,1)S(1)}, bf16[128,1616]{0,1:T(8,128)(2,1)S(1)}, u32[]{:S(2)}, u32[]{:S(2)}) collective-permute-start(bf16[128,1616]{0,1:T(8,128)(2,1)S(1)} %collective-permute-done.1), channel_id=1, source_target_pairs={{0,7},{1,0},{2,1},{3,2},{4,3},{5,4},{6,5},{7,6},{8,15},{9,8},{10,9... | collective-permute-start | bytes 1241096 | tf_op jit(solution)/shard_map/ppermute | solution.py:21
  46.1 0.9 slice_dynamic-update-slice_fusion.5
  47.0 2.9 %collective-permute-done.5 = bf16[128,1616]{0,1:T(8,128)(2,1)S(1)} collective-permute-done((bf16[128,1616]{0,1:T(8,128)(2,1)S(1)}, bf16[128,1616]{0,1:T(8,128)(2,1)S(1)}, u32[]{:S(2)}, u32[]{:S(2)}) %collective-permute-start.5) | collective-permute-done | bytes 413728 | tf_op jit(solution)/shard_map/ppermute | solution.py:21
  50.0 2.1 %collective-permute-start.6 = (bf16[128,1616]{0,1:T(8,128)(2,1)S(1)}, bf16[128,1616]{0,1:T(8,128)(2,1)S(1)}, u32[]{:S(2)}, u32[]{:S(2)}) collective-permute-start(bf16[128,1616]{0,1:T(8,128)(2,1)S(1)} %collective-permute-done.5), channel_id=1, source_target_pairs={{0,1},{1,2},{2,3},{3,4},{4,5},{5,6},{6,7},{7,0},{8,9},{9,10},{10,1... | collective-permute-start | bytes 1241096 | tf_op jit(solution)/shard_map/ppermute | solution.py:21
  52.1 2.0 %collective-permute-done.2 = bf16[128,1616]{0,1:T(8,128)(2,1)S(1)} collective-permute-done((bf16[128,1616]{0,1:T(8,128)(2,1)S(1)}, bf16[128,1616]{0,1:T(8,128)(2,1)S(1)}, u32[]{:S(2)}, u32[]{:S(2)}) %collective-permute-start.2) | collective-permute-done | bytes 413728 | tf_op jit(solution)/shard_map/ppermute | solution.py:21
  54.1 0.8 slice_dynamic-update-slice_fusion.4
  54.9 5.5 %collective-permute-done.6 = bf16[128,1616]{0,1:T(8,128)(2,1)S(1)} collective-permute-done((bf16[128,1616]{0,1:T(8,128)(2,1)S(1)}, bf16[128,1616]{0,1:T(8,128)(2,1)S(1)}, u32[]{:S(2)}, u32[]{:S(2)}) %collective-permute-start.6) | collective-permute-done | bytes 413728 | tf_op jit(solution)/shard_map/ppermute | solution.py:21
  60.5 0.8 slice_dynamic-update-slice_fusion.3
  61.4 0.9 slice_dynamic-update-slice_fusion.2
  62.2 0.8 slice_dynamic-update-slice_fusion.1
  63.1 0.9 slice_dynamic-update-slice_fusion
  63.9 40.9 %all-gather.2.cloned.1.call-done = bf16[2048,1600]{1,0:T(8,128)(2,1)} async-done(((bf16[32,1600]{1,0:T(8,128)(2,1)}), bf16[2048,1600]{1,0:T(8,128)(2,1)}) %all-gather.2.cloned.1.call-update) | async-done | bytes 6553616 | tf_op jit(solution)/shard_map/all_gather | solution.py:67
  104.8 4.7 %fusion.82 = (f32[1024]{0:T(1024)S(1)}, f32[1024,512]{0,1:T(8,128)S(1)}) fusion(bf16[1024,1600]{0,1:T(8,128)(2,1)} %slice_dynamic-update-slice_fusion, bf16[2048,1600]{1,0:T(8,128)(2,1)} %all-gather.2.cloned.1.call-done), kind=kOutput, calls=%fused_computation.177 | convolution fusion | flops 1678244864 | bytes 7081984 | tf_op jit(solution)/shard_map/dot_general | solution.py:25
  109.5 2.1 %fusion.83 = (f32[1024]{0:T(1024)S(1)}, f32[1024,512]{0,1:T(8,128)S(1)}) fusion(bf16[1024,1600]{0,1:T(8,128)(2,1)S(1)} %copy-done, bf16[2048,1600]{1,0:T(8,128)(2,1)S(1)} %copy-done.2), kind=kOutput, calls=%fused_computation.178 | convolution fusion | flops 1678244864 | bytes 7081984 | tf_op jit(solution)/shard_map/dot_general | solution.py:25
  111.7 2.1 %fusion.84 = (f32[1024]{0:T(1024)S(1)}, f32[1024,512]{0,1:T(8,128)S(1)}) fusion(bf16[1024,1600]{0,1:T(8,128)(2,1)S(1)} %copy-done, bf16[2048,1600]{1,0:T(8,128)(2,1)S(1)} %copy-done.2), kind=kOutput, calls=%fused_computation.179 | convolution fusion | flops 1678244864 | bytes 7081984 | tf_op jit(solution)/shard_map/dot_general | solution.py:25
  113.8 2.1 %fusion.85 = (f32[1024]{0:T(1024)S(1)}, f32[1024,512]{0,1:T(8,128)S(1)}) fusion(bf16[1024,1600]{0,1:T(8,128)(2,1)S(1)} %copy-done, bf16[2048,1600]{1,0:T(8,128)(2,1)S(1)} %copy-done.2), kind=kOutput, calls=%fused_computation.180 | convolution fusion | flops 1678244864 | bytes 7081984 | tf_op jit(solution)/shard_map/dot_general | solution.py:25
  115.9 3.9 %fusion = (f32[1024]{0:T(1024)S(1)}, f32[1024]{0:T(1024)S(1)}, f32[1024]{0:T(1024)S(1)}, f32[1024]{0:T(1024)S(1)}, f32[1024]{0:T(1024)S(1)}, /*index=5*/f32[1024...) fusion(f32[1024,512]{0,1:T(8,128)S(1)} %get-tuple-element.67, ...), kind=kLoop, calls=%fused_computation.8 | loop fusion | flops 14667776 | bytes 8466432 | tf_op jit(solution)/shard_map/reduce_sum | solution.py:32
  119.9 12.9 %all_to_all.6 = f32[4,8,128]{2,0,1:T(4,128)S(1)} all-to-all(f32[4,8,128]{2,0,1:T(4,128)S(1)} %copy.9), channel_id=1, replica_groups=mesh['z'=8,'x'=4,'c'=2,'y'=8] {'y'}, dimensions={1} | all-to-all | bytes 32768 | tf_op jit(solution)/shard_map/all_to_all | solution.py:79
  (32 shorter events, 0.9 us)
Async XLA Ops:
  7.2 97.7 %all-gather.2.cloned.1.call-start = ((), (), s32[]{:S(2)}) async-start(), calls=%async_computation.1 | async-start | bytes 6922240 | tf_op jit(solution)/shard_map/all_gather | solution.py:67
  14.6 11.3 %collective-permute-start.3 = (bf16[128,1616]{0,1:T(8,128)(2,1)S(1)}, bf16[128,1616]{0,1:T(8,128)(2,1)S(1)}, u32[]{:S(2)}, u32[]{:S(2)}) collective-permute-start(bf16[128,1616]{0,1:T(8,128)(2,1)S(1)} %pad_maximum_fusion), channel_id=1, source_target_pairs={{0,1},{1,2},{2,3},{3,4},{4,5},{5,6},{6,7},{7,0},{8,9},{9,10},{10,1... | collective-permute-start | bytes 1241096 | tf_op jit(solution)/shard_map/ppermute | solution.py:21
  18.6 11.4 %collective-permute-start = (bf16[128,1616]{0,1:T(8,128)(2,1)S(1)}, bf16[128,1616]{0,1:T(8,128)(2,1)S(1)}, u32[]{:S(2)}, u32[]{:S(2)}) collective-permute-start(bf16[128,1616]{0,1:T(8,128)(2,1)S(1)} %pad_maximum_fusion), channel_id=1, source_target_pairs={{0,7},{1,0},{2,1},{3,2},{4,3},{5,4},{6,5},{7,6},{8,15},{9,8},{10,9... | collective-permute-start | bytes 1241096 | tf_op jit(solution)/shard_map/ppermute | solution.py:21
  25.9 12.6 %collective-permute-start.4 = (bf16[128,1616]{0,1:T(8,128)(2,1)S(1)}, bf16[128,1616]{0,1:T(8,128)(2,1)S(1)}, u32[]{:S(2)}, u32[]{:S(2)}) collective-permute-start(bf16[128,1616]{0,1:T(8,128)(2,1)S(1)} %collective-permute-done.3), channel_id=1, source_target_pairs={{0,1},{1,2},{2,3},{3,4},{4,5},{5,6},{6,7},{7,0},{8,9},{9,10},{10,1... | collective-permute-start | bytes 1241096 | tf_op jit(solution)/shard_map/ppermute | solution.py:21
  30.0 11.4 %collective-permute-start.1 = (bf16[128,1616]{0,1:T(8,128)(2,1)S(1)}, bf16[128,1616]{0,1:T(8,128)(2,1)S(1)}, u32[]{:S(2)}, u32[]{:S(2)}) collective-permute-start(bf16[128,1616]{0,1:T(8,128)(2,1)S(1)} %collective-permute-done), channel_id=1, source_target_pairs={{0,7},{1,0},{2,1},{3,2},{4,3},{5,4},{6,5},{7,6},{8,15},{9,8},{10,9... | collective-permute-start | bytes 1241096 | tf_op jit(solution)/shard_map/ppermute | solution.py:21
  38.5 11.5 %collective-permute-start.5 = (bf16[128,1616]{0,1:T(8,128)(2,1)S(1)}, bf16[128,1616]{0,1:T(8,128)(2,1)S(1)}, u32[]{:S(2)}, u32[]{:S(2)}) collective-permute-start(bf16[128,1616]{0,1:T(8,128)(2,1)S(1)} %collective-permute-done.4), channel_id=1, source_target_pairs={{0,1},{1,2},{2,3},{3,4},{4,5},{5,6},{6,7},{7,0},{8,9},{9,10},{10,1... | collective-permute-start | bytes 1241096 | tf_op jit(solution)/shard_map/ppermute | solution.py:21
  41.4 12.7 %collective-permute-start.2 = (bf16[128,1616]{0,1:T(8,128)(2,1)S(1)}, bf16[128,1616]{0,1:T(8,128)(2,1)S(1)}, u32[]{:S(2)}, u32[]{:S(2)}) collective-permute-start(bf16[128,1616]{0,1:T(8,128)(2,1)S(1)} %collective-permute-done.1), channel_id=1, source_target_pairs={{0,7},{1,0},{2,1},{3,2},{4,3},{5,4},{6,5},{7,6},{8,15},{9,8},{10,9... | collective-permute-start | bytes 1241096 | tf_op jit(solution)/shard_map/ppermute | solution.py:21
  50.0 10.5 %collective-permute-start.6 = (bf16[128,1616]{0,1:T(8,128)(2,1)S(1)}, bf16[128,1616]{0,1:T(8,128)(2,1)S(1)}, u32[]{:S(2)}, u32[]{:S(2)}) collective-permute-start(bf16[128,1616]{0,1:T(8,128)(2,1)S(1)} %collective-permute-done.5), channel_id=1, source_target_pairs={{0,1},{1,2},{2,3},{3,4},{4,5},{5,6},{6,7},{7,0},{8,9},{9,10},{10,1... | collective-permute-start | bytes 1241096 | tf_op jit(solution)/shard_map/ppermute | solution.py:21
  63.9 45.6 %copy-start = (bf16[1024,1600]{0,1:T(8,128)(2,1)S(1)}, bf16[1024,1600]{0,1:T(8,128)(2,1)}, u32[]{:S(2)}) copy-start(bf16[1024,1600]{0,1:T(8,128)(2,1)} %slice_dynamic-update-slice_fusion) | copy-start | bytes 9830404
  104.8 4.7 %copy-start.2 = (bf16[2048,1600]{1,0:T(8,128)(2,1)S(1)}, bf16[2048,1600]{1,0:T(8,128)(2,1)}, u32[]{:S(2)}) copy-start(bf16[2048,1600]{1,0:T(8,128)(2,1)} %all-gather.2.cloned.1.call-done) | copy-start | bytes 19660804
  115.9 17.0 %copy-start.1 = (s32[128]{0:T(128)S(1)}, s32[128]{0:T(128)}, u32[]{:S(2)}) copy-start(s32[128]{0:T(128)} %param.13) | copy-start | bytes 1540
Sparse Core Ops, SparseCore 0:
  11.3 93.4 all-gather.1
where the time goes:
time: 141 us; the launch traced here: 140 us
  waiting for transfers between devices  58.4 us (41%)
  starting transfers between devices  26.4 us (19%)
  between operations  14.3 us (10%)
  blocking collectives  12.9 us (9%)
  other arithmetic  11.3 us (8%)
  matrix products  11 us (8%)
  local copies, waits for them, and re-layouts  5.97 us (4%)
    all_gather x1, waiting for transfers between devices, on_device(): whole = lax.all_gather(unembed, ('z', 'x', 'c'), axis=0, tiled=True)  40.9 us
    ppermute x7, starting transfers between devices, shift(): lax.ppermute(value, axis, [(i, (i + step) % size) for i in range(size)])  26.4 us
    ppermute x7, waiting for transfers between devices, shift(): lax.ppermute(value, axis, [(i, (i + step) % size) for i in range(size)])  16.8 us
    all_to_all x1, blocking collectives, on_device(): got = lax.all_to_all(packed, 'y', 1, 1, tiled=True).reshape(4, ny, mine)  12.9 us
    dot_general x4, matrix products, chunk_stats(): lax.dot_general(normed, piece, (((1,), (1,)), ((), ())), preferred_elemen...  11 us
    unnamed x12, local copies, waits for them, and re-layouts  5.05 us
    reduce_sum x1, other arithmetic, chunk_stats(): jnp.sum(weights * shifted, axis=1)  3.9 us
  transfers between devices with their start and end apart: 8, of which 6 were waited for; matrix products, arithmetic and copies ran while one was open for 9% of the time, Pallas kernels for 0%

commit v1 on v0

--- a/solution.py
+++ b/solution.py
@@ -76,7 +76,9 @@
             stats, chunk_stats(rows, whole[first : first + step], ids[first : first + step], wanted)
         )
     packed = jnp.roll(jnp.stack(stats).reshape(4, ny, mine), y, axis=1).reshape(4, ny * mine)
-    got = lax.all_to_all(packed, "y", 1, 1, tiled=True).reshape(4, ny, mine)
+    got = jnp.concatenate(
+        lax.all_to_all(jnp.stack(jnp.split(packed, lax.axis_size("y"), axis=1)), "y", 0, 0), axis=1
+    ).reshape(4, ny, mine)
     tops, totals, spreads, chosen = (got[0], got[1], got[2], got[3])
     top = jnp.max(tops, axis=0)
     scale = jnp.exp(tops - top[None])

time: 141 us -> 141 us (level)
    unnamed x12 -> x20, local copies, waits for them, and re-layouts: 5.05 us -> 5.12 us
where the time goes in v1:
time: 141 us; the launch traced here: 140 us
  waiting for transfers between devices  58.4 us (41%)
  starting transfers between devices  26.4 us (19%)
  between operations  14.3 us (10%)
  blocking collectives  12.9 us (9%)
  other arithmetic  11.3 us (8%)
  matrix products  11 us (8%)
  local copies, waits for them, and re-layouts  6.04 us (4%)
    all_gather x1, waiting for transfers between devices, on_device(): whole = lax.all_gather(unembed, ('z', 'x', 'c'), axis=0, tiled=True)  40.9 us
    ppermute x7, starting transfers between devices, shift(): lax.ppermute(value, axis, [(i, (i + step) % size) for i in range(size)])  26.4 us
    ppermute x7, waiting for transfers between devices, shift(): lax.ppermute(value, axis, [(i, (i + step) % size) for i in range(size)])  16.8 us
    all_to_all x1, blocking collectives, on_device(): lax.all_to_all(jnp.stack(jnp.split(packed, lax.axis_size('y'), axis=1)),...  12.9 us
    dot_general x4, matrix products, chunk_stats(): lax.dot_general(normed, piece, (((1,), (1,)), ((), ())), preferred_elemen...  11 us
    unnamed x20, local copies, waits for them, and re-layouts  5.12 us
    reduce_sum x1, other arithmetic, chunk_stats(): jnp.sum(weights * shifted, axis=1)  3.9 us
  transfers between devices with their start and end apart: 8, of which 6 were waited for; matrix products, arithmetic and copies ran while one was open for 9% of the time, Pallas kernels for 0%

profile of v1, /device:TPU:1, one launch (start us, length us, event | category | flops | bytes accessed | tf_op | source)
XLA Modules:
  0.0 140.3 jit_solution(7402019807284296262)
XLA Ops:
  7.2 0.7 all-gather.2.cloned.1.call-update
  7.9 0.6 compare_reduce_fusion.1
  8.5 0.6 compare_reduce_fusion
  9.2 2.0 %broadcast_select_fusion = (bf16[128]{0:T(256)(128)(2,1)S(1)}, bf16[128,1]{0,1:T(2,128)(2,1)S(1)}) fusion(pred[]{:T(512)} %compare_reduce_fusion, s32[128]{0:T(128)} %param.12, pred[]{:T(512)} %compare_reduce_fusion.1), kind=kLoop, calls=%fused_computation.146 | loop fusion | flops 2944 | bytes 1026 | tf_op jit(solution)/shard_map/slice | solution.py:64
  11.2 1.2 fusion.12
  12.4 2.1 %constant_dynamic-update-slice_fusion = (bf16[1024,1600]{0,1:T(8,128)(2,1)}, bf16[128,1600]{0,1:T(8,128)(2,1)S(1)}) fusion(f32[1600]{0:T(1024)} %param.10, f32[128]{0:T(128)S(1)} %add_rsqrt_fusion, bf16[128,1600]{0,1:T(8,128)(2,1)} %param.9), kind=kLoop, calls=%fused_computation.37 | loop fusion | flops 819199 | bytes 1235712
  14.6 4.0 %collective-permute-start.3 = (bf16[128,1616]{0,1:T(8,128)(2,1)S(1)}, bf16[128,1616]{0,1:T(8,128)(2,1)S(1)}, u32[]{:S(2)}, u32[]{:S(2)}) collective-permute-start(bf16[128,1616]{0,1:T(8,128)(2,1)S(1)} %pad_maximum_fusion), channel_id=1, source_target_pairs={{0,1},{1,2},{2,3},{3,4},{4,5},{5,6},{6,7},{7,0},{8,9},{9,10},{10,1... | collective-permute-start | bytes 1241096 | tf_op jit(solution)/shard_map/ppermute | solution.py:21
  18.6 3.8 %collective-permute-start = (bf16[128,1616]{0,1:T(8,128)(2,1)S(1)}, bf16[128,1616]{0,1:T(8,128)(2,1)S(1)}, u32[]{:S(2)}, u32[]{:S(2)}) collective-permute-start(bf16[128,1616]{0,1:T(8,128)(2,1)S(1)} %pad_maximum_fusion), channel_id=1, source_target_pairs={{0,7},{1,0},{2,1},{3,2},{4,3},{5,4},{6,5},{7,6},{8,15},{9,8},{10,9... | collective-permute-start | bytes 1241096 | tf_op jit(solution)/shard_map/ppermute | solution.py:21
  22.5 3.4 %collective-permute-done.3 = bf16[128,1616]{0,1:T(8,128)(2,1)S(1)} collective-permute-done((bf16[128,1616]{0,1:T(8,128)(2,1)S(1)}, bf16[128,1616]{0,1:T(8,128)(2,1)S(1)}, u32[]{:S(2)}, u32[]{:S(2)}) %collective-permute-start.3) | collective-permute-done | bytes 413728 | tf_op jit(solution)/shard_map/ppermute | solution.py:21
  25.9 4.1 %collective-permute-start.4 = (bf16[128,1616]{0,1:T(8,128)(2,1)S(1)}, bf16[128,1616]{0,1:T(8,128)(2,1)S(1)}, u32[]{:S(2)}, u32[]{:S(2)}) collective-permute-start(bf16[128,1616]{0,1:T(8,128)(2,1)S(1)} %collective-permute-done.3), channel_id=1, source_target_pairs={{0,1},{1,2},{2,3},{3,4},{4,5},{5,6},{6,7},{7,0},{8,9},{9,10},{10,1... | collective-permute-start | bytes 1241096 | tf_op jit(solution)/shard_map/ppermute | solution.py:21
  30.0 4.7 %collective-permute-start.1 = (bf16[128,1616]{0,1:T(8,128)(2,1)S(1)}, bf16[128,1616]{0,1:T(8,128)(2,1)S(1)}, u32[]{:S(2)}, u32[]{:S(2)}) collective-permute-start(bf16[128,1616]{0,1:T(8,128)(2,1)S(1)} %collective-permute-done), channel_id=1, source_target_pairs={{0,7},{1,0},{2,1},{3,2},{4,3},{5,4},{6,5},{7,6},{8,15},{9,8},{10,9... | collective-permute-start | bytes 1241096 | tf_op jit(solution)/shard_map/ppermute | solution.py:21
  34.8 0.8 slice_dynamic-update-slice_fusion.6
  35.6 2.9 %collective-permute-done.4 = bf16[128,1616]{0,1:T(8,128)(2,1)S(1)} collective-permute-done((bf16[128,1616]{0,1:T(8,128)(2,1)S(1)}, bf16[128,1616]{0,1:T(8,128)(2,1)S(1)}, u32[]{:S(2)}, u32[]{:S(2)}) %collective-permute-start.4) | collective-permute-done | bytes 413728 | tf_op jit(solution)/shard_map/ppermute | solution.py:21
  38.5 2.9 %collective-permute-start.5 = (bf16[128,1616]{0,1:T(8,128)(2,1)S(1)}, bf16[128,1616]{0,1:T(8,128)(2,1)S(1)}, u32[]{:S(2)}, u32[]{:S(2)}) collective-permute-start(bf16[128,1616]{0,1:T(8,128)(2,1)S(1)} %collective-permute-done.4), channel_id=1, source_target_pairs={{0,1},{1,2},{2,3},{3,4},{4,5},{5,6},{6,7},{7,0},{8,9},{9,10},{10,1... | collective-permute-start | bytes 1241096 | tf_op jit(solution)/shard_map/ppermute | solution.py:21
  41.4 4.7 %collective-permute-start.2 = (bf16[128,1616]{0,1:T(8,128)(2,1)S(1)}, bf16[128,1616]{0,1:T(8,128)(2,1)S(1)}, u32[]{:S(2)}, u32[]{:S(2)}) collective-permute-start(bf16[128,1616]{0,1:T(8,128)(2,1)S(1)} %collective-permute-done.1), channel_id=1, source_target_pairs={{0,7},{1,0},{2,1},{3,2},{4,3},{5,4},{6,5},{7,6},{8,15},{9,8},{10,9... | collective-permute-start | bytes 1241096 | tf_op jit(solution)/shard_map/ppermute | solution.py:21
  46.1 0.9 slice_dynamic-update-slice_fusion.5
  47.0 2.9 %collective-permute-done.5 = bf16[128,1616]{0,1:T(8,128)(2,1)S(1)} collective-permute-done((bf16[128,1616]{0,1:T(8,128)(2,1)S(1)}, bf16[128,1616]{0,1:T(8,128)(2,1)S(1)}, u32[]{:S(2)}, u32[]{:S(2)}) %collective-permute-start.5) | collective-permute-done | bytes 413728 | tf_op jit(solution)/shard_map/ppermute | solution.py:21
  50.0 2.1 %collective-permute-start.6 = (bf16[128,1616]{0,1:T(8,128)(2,1)S(1)}, bf16[128,1616]{0,1:T(8,128)(2,1)S(1)}, u32[]{:S(2)}, u32[]{:S(2)}) collective-permute-start(bf16[128,1616]{0,1:T(8,128)(2,1)S(1)} %collective-permute-done.5), channel_id=1, source_target_pairs={{0,1},{1,2},{2,3},{3,4},{4,5},{5,6},{6,7},{7,0},{8,9},{9,10},{10,1... | collective-permute-start | bytes 1241096 | tf_op jit(solution)/shard_map/ppermute | solution.py:21
  52.1 2.0 %collective-permute-done.2 = bf16[128,1616]{0,1:T(8,128)(2,1)S(1)} collective-permute-done((bf16[128,1616]{0,1:T(8,128)(2,1)S(1)}, bf16[128,1616]{0,1:T(8,128)(2,1)S(1)}, u32[]{:S(2)}, u32[]{:S(2)}) %collective-permute-start.2) | collective-permute-done | bytes 413728 | tf_op jit(solution)/shard_map/ppermute | solution.py:21
  54.1 0.8 slice_dynamic-update-slice_fusion.4
  54.9 5.5 %collective-permute-done.6 = bf16[128,1616]{0,1:T(8,128)(2,1)S(1)} collective-permute-done((bf16[128,1616]{0,1:T(8,128)(2,1)S(1)}, bf16[128,1616]{0,1:T(8,128)(2,1)S(1)}, u32[]{:S(2)}, u32[]{:S(2)}) %collective-permute-start.6) | collective-permute-done | bytes 413728 | tf_op jit(solution)/shard_map/ppermute | solution.py:21
  60.5 0.8 slice_dynamic-update-slice_fusion.3
  61.4 0.9 slice_dynamic-update-slice_fusion.2
  62.2 0.8 slice_dynamic-update-slice_fusion.1
  63.1 0.9 slice_dynamic-update-slice_fusion
  63.9 40.9 %all-gather.2.cloned.1.call-done = bf16[2048,1600]{1,0:T(8,128)(2,1)} async-done(((bf16[32,1600]{1,0:T(8,128)(2,1)}), bf16[2048,1600]{1,0:T(8,128)(2,1)}) %all-gather.2.cloned.1.call-update) | async-done | bytes 6553616 | tf_op jit(solution)/shard_map/all_gather | solution.py:67
  104.8 4.7 %fusion.83 = (f32[1024]{0:T(1024)S(1)}, f32[1024,512]{0,1:T(8,128)S(1)}) fusion(bf16[1024,1600]{0,1:T(8,128)(2,1)} %slice_dynamic-update-slice_fusion, bf16[2048,1600]{1,0:T(8,128)(2,1)} %all-gather.2.cloned.1.call-done), kind=kOutput, calls=%fused_computation.195 | convolution fusion | flops 1678244864 | bytes 7081984 | tf_op jit(solution)/shard_map/dot_general | solution.py:25
  109.5 2.1 %fusion.84 = (f32[1024]{0:T(1024)S(1)}, f32[1024,512]{0,1:T(8,128)S(1)}) fusion(bf16[1024,1600]{0,1:T(8,128)(2,1)S(1)} %copy-done, bf16[2048,1600]{1,0:T(8,128)(2,1)S(1)} %copy-done.2), kind=kOutput, calls=%fused_computation.196 | convolution fusion | flops 1678244864 | bytes 7081984 | tf_op jit(solution)/shard_map/dot_general | solution.py:25
  111.7 2.1 %fusion.85 = (f32[1024]{0:T(1024)S(1)}, f32[1024,512]{0,1:T(8,128)S(1)}) fusion(bf16[1024,1600]{0,1:T(8,128)(2,1)S(1)} %copy-done, bf16[2048,1600]{1,0:T(8,128)(2,1)S(1)} %copy-done.2), kind=kOutput, calls=%fused_computation.197 | convolution fusion | flops 1678244864 | bytes 7081984 | tf_op jit(solution)/shard_map/dot_general | solution.py:25
  113.8 2.1 %fusion.86 = (f32[1024]{0:T(1024)S(1)}, f32[1024,512]{0,1:T(8,128)S(1)}) fusion(bf16[1024,1600]{0,1:T(8,128)(2,1)S(1)} %copy-done, bf16[2048,1600]{1,0:T(8,128)(2,1)S(1)} %copy-done.2), kind=kOutput, calls=%fused_computation.198 | convolution fusion | flops 1678244864 | bytes 7081984 | tf_op jit(solution)/shard_map/dot_general | solution.py:25
  115.9 3.9 %fusion = (f32[1024]{0:T(1024)S(1)}, f32[1024]{0:T(1024)S(1)}, f32[1024]{0:T(1024)S(1)}, f32[1024]{0:T(1024)S(1)}, f32[1024]{0:T(1024)S(1)}, /*index=5*/f32[1024...) fusion(f32[1024,512]{0,1:T(8,128)S(1)} %get-tuple-element.67, ...), kind=kLoop, calls=%fused_computation.8 | loop fusion | flops 14667776 | bytes 8466432 | tf_op jit(solution)/shard_map/reduce_sum | solution.py:32
  120.0 12.9 %all_to_all.5 = f32[8,4,128]{2,1,0:T(4,128)S(1)} all-to-all(f32[8,4,128]{2,1,0:T(4,128)S(1)} %constant_dynamic-update-slice_fusion.2), channel_id=1, replica_groups=mesh['z'=8,'x'=4,'c'=2,'y'=8] {'y'}, dimensions={0} | all-to-all | bytes 32768 | tf_op jit(solution)/shard_map/all_to_all | solution.py:80
  (40 shorter events, 1.0 us)
Async XLA Ops:
  7.2 97.7 %all-gather.2.cloned.1.call-start = ((), (), s32[]{:S(2)}) async-start(), calls=%async_computation.1 | async-start | bytes 6922240 | tf_op jit(solution)/shard_map/all_gather | solution.py:67
  14.6 11.3 %collective-permute-start.3 = (bf16[128,1616]{0,1:T(8,128)(2,1)S(1)}, bf16[128,1616]{0,1:T(8,128)(2,1)S(1)}, u32[]{:S(2)}, u32[]{:S(2)}) collective-permute-start(bf16[128,1616]{0,1:T(8,128)(2,1)S(1)} %pad_maximum_fusion), channel_id=1, source_target_pairs={{0,1},{1,2},{2,3},{3,4},{4,5},{5,6},{6,7},{7,0},{8,9},{9,10},{10,1... | collective-permute-start | bytes 1241096 | tf_op jit(solution)/shard_map/ppermute | solution.py:21
  18.6 11.4 %collective-permute-start = (bf16[128,1616]{0,1:T(8,128)(2,1)S(1)}, bf16[128,1616]{0,1:T(8,128)(2,1)S(1)}, u32[]{:S(2)}, u32[]{:S(2)}) collective-permute-start(bf16[128,1616]{0,1:T(8,128)(2,1)S(1)} %pad_maximum_fusion), channel_id=1, source_target_pairs={{0,7},{1,0},{2,1},{3,2},{4,3},{5,4},{6,5},{7,6},{8,15},{9,8},{10,9... | collective-permute-start | bytes 1241096 | tf_op jit(solution)/shard_map/ppermute | solution.py:21
  25.9 12.6 %collective-permute-start.4 = (bf16[128,1616]{0,1:T(8,128)(2,1)S(1)}, bf16[128,1616]{0,1:T(8,128)(2,1)S(1)}, u32[]{:S(2)}, u32[]{:S(2)}) collective-permute-start(bf16[128,1616]{0,1:T(8,128)(2,1)S(1)} %collective-permute-done.3), channel_id=1, source_target_pairs={{0,1},{1,2},{2,3},{3,4},{4,5},{5,6},{6,7},{7,0},{8,9},{9,10},{10,1... | collective-permute-start | bytes 1241096 | tf_op jit(solution)/shard_map/ppermute | solution.py:21
  30.0 11.4 %collective-permute-start.1 = (bf16[128,1616]{0,1:T(8,128)(2,1)S(1)}, bf16[128,1616]{0,1:T(8,128)(2,1)S(1)}, u32[]{:S(2)}, u32[]{:S(2)}) collective-permute-start(bf16[128,1616]{0,1:T(8,128)(2,1)S(1)} %collective-permute-done), channel_id=1, source_target_pairs={{0,7},{1,0},{2,1},{3,2},{4,3},{5,4},{6,5},{7,6},{8,15},{9,8},{10,9... | collective-permute-start | bytes 1241096 | tf_op jit(solution)/shard_map/ppermute | solution.py:21
  38.5 11.5 %collective-permute-start.5 = (bf16[128,1616]{0,1:T(8,128)(2,1)S(1)}, bf16[128,1616]{0,1:T(8,128)(2,1)S(1)}, u32[]{:S(2)}, u32[]{:S(2)}) collective-permute-start(bf16[128,1616]{0,1:T(8,128)(2,1)S(1)} %collective-permute-done.4), channel_id=1, source_target_pairs={{0,1},{1,2},{2,3},{3,4},{4,5},{5,6},{6,7},{7,0},{8,9},{9,10},{10,1... | collective-permute-start | bytes 1241096 | tf_op jit(solution)/shard_map/ppermute | solution.py:21
  41.4 12.7 %collective-permute-start.2 = (bf16[128,1616]{0,1:T(8,128)(2,1)S(1)}, bf16[128,1616]{0,1:T(8,128)(2,1)S(1)}, u32[]{:S(2)}, u32[]{:S(2)}) collective-permute-start(bf16[128,1616]{0,1:T(8,128)(2,1)S(1)} %collective-permute-done.1), channel_id=1, source_target_pairs={{0,7},{1,0},{2,1},{3,2},{4,3},{5,4},{6,5},{7,6},{8,15},{9,8},{10,9... | collective-permute-start | bytes 1241096 | tf_op jit(solution)/shard_map/ppermute | solution.py:21
  50.0 10.5 %collective-permute-start.6 = (bf16[128,1616]{0,1:T(8,128)(2,1)S(1)}, bf16[128,1616]{0,1:T(8,128)(2,1)S(1)}, u32[]{:S(2)}, u32[]{:S(2)}) collective-permute-start(bf16[128,1616]{0,1:T(8,128)(2,1)S(1)} %collective-permute-done.5), channel_id=1, source_target_pairs={{0,1},{1,2},{2,3},{3,4},{4,5},{5,6},{6,7},{7,0},{8,9},{9,10},{10,1... | collective-permute-start | bytes 1241096 | tf_op jit(solution)/shard_map/ppermute | solution.py:21
  63.9 45.6 %copy-start = (bf16[1024,1600]{0,1:T(8,128)(2,1)S(1)}, bf16[1024,1600]{0,1:T(8,128)(2,1)}, u32[]{:S(2)}) copy-start(bf16[1024,1600]{0,1:T(8,128)(2,1)} %slice_dynamic-update-slice_fusion) | copy-start | bytes 9830404
  104.8 4.7 %copy-start.2 = (bf16[2048,1600]{1,0:T(8,128)(2,1)S(1)}, bf16[2048,1600]{1,0:T(8,128)(2,1)}, u32[]{:S(2)}) copy-start(bf16[2048,1600]{1,0:T(8,128)(2,1)} %all-gather.2.cloned.1.call-done) | copy-start | bytes 19660804
  115.9 17.1 %copy-start.1 = (s32[128]{0:T(128)S(1)}, s32[128]{0:T(128)}, u32[]{:S(2)}) copy-start(s32[128]{0:T(128)} %param.13) | copy-start | bytes 1540
Sparse Core Ops, SparseCore 0:
  11.3 93.4 all-gather.1
